TPU v7x, 512 devices: a whole 4x8x8 slice. The times are simulated.
512 devices in a mesh: dp: 16 (over z, core), expert: 32 (over x, y).
Axes of the slice: x: 4, y: 8, z: 8, core: 2. Of those that a mesh axis runs over, the one named last changes fastest.
Arguments:
- out_grad: bfloat16 [65536, 1024], P(('dp', 'expert')), may hold values from -6 to 6
- hidden: bfloat16 [65536, 8, 384], P(('dp', 'expert')), may hold values from -1.5 to 1.5
- gate: bfloat16 [65536, 8], P(('dp', 'expert')), may hold values from 0.049804688 to 0.5
- route_expert: int32 [65536, 8], P(('dp', 'expert')), may hold values from 0 to 63, as said below
- route_replica: int32 [65536, 8], P(('dp', 'expert')), may hold values from 0 to 3, as said below
- slot_expert: int32 [32, 3], replicated, may hold values from 0 to 63, as said below
- down_weight: bfloat16 [32, 3, 384, 1024], P('expert')
Outputs:
- d_hidden: bfloat16 [65536, 8, 384], P(('dp', 'expert'))
- d_gate: bfloat16 [65536, 8], P(('dp', 'expert'))
- d_weight: float32 [32, 3, 384, 1024], P('expert', None, 'dp')
Inputs may be any that keep to these rules, and one draw needn't show every extreme that they name: `slot_expert`: every expert holds 1 to 4 slots: exactly 8 experts hold 4, 8 hold 2, the rest 1. `route_expert`: the 8 experts of a token differ. Of the routes of one device's 128 tokens, at most 16 go to one slot, and some slot receives exactly 16 routes from every device. route_replica is below the number of slots of the route's expert.
All inputs are finite; a program needn't handle non-finite values.
Results may differ from a plain program's by a relative error of at most 0.0029.
Values may be sent and summed in bfloat16 or wider, within the bound.
No kernel may reach another device: no remote copies, remote signals or barrier semaphores. Data moves between devices by JAX's collectives and lax.ppermute only.
A program may use at most 128 MiB of HBM per device.

v0:
```python
import jax
import jax.numpy as jnp
from jax import lax
from jax.sharding import PartitionSpec as P

EXPERTS = 64
CAP = 16
HOT = 16


def slot_of_route(experts, replicas, flat_slots):
    slot_count = flat_slots.shape[0]
    ordering = jnp.arange(slot_count, dtype=jnp.int32)
    same_expert = flat_slots[:, None] == flat_slots[None, :]
    replica_rank = jnp.sum(
        (same_expert & (ordering[None, :] < ordering[:, None])).astype(jnp.int32), axis=1
    )
    matches = (experts.reshape(-1)[:, None] == flat_slots[None, :]) & (
        replicas.reshape(-1)[:, None] == replica_rank[None, :]
    )
    return jnp.sum(jnp.where(matches, ordering[None, :], 0), axis=1)


def buffer_places(experts, replicas, flat_slots, capacity):
    destination = slot_of_route(experts, replicas, flat_slots)
    slot_count = flat_slots.shape[0]
    onehot = (destination[:, None] == jnp.arange(slot_count, dtype=jnp.int32)[None, :]).astype(
        jnp.int32
    )
    before = jnp.cumsum(onehot, axis=0) - onehot
    position = jnp.sum(before * onehot, axis=1)
    return destination * capacity + position


def route_of_place(places, length):
    route_count = places.shape[0]
    return (
        jnp.full((length,), route_count, jnp.int32)
        .at[places]
        .set(jnp.arange(route_count, dtype=jnp.int32))
    )


def per_device(out_grad, hidden, gate, route_expert, route_replica, slot_expert, down_weight):
    tok_rows, chosen_count = gate.shape
    model_width = out_grad.shape[1]
    hidden_width = hidden.shape[2]
    groups, slots = slot_expert.shape
    flat_slots = slot_expert.reshape(-1)
    capacity = CAP
    block_rows = slots * capacity
    length = groups * block_rows
    route_count = tok_rows * chosen_count
    own_index = lax.axis_index("expert")
    places = buffer_places(route_expert, route_replica, flat_slots, capacity)
    source_route = route_of_place(places, length)
    hidden_rows = jnp.concatenate(
        [hidden.reshape(route_count, hidden_width), jnp.zeros((1, hidden_width), hidden.dtype)],
        axis=0,
    )
    gate_rows = jnp.concatenate([gate.reshape(route_count), jnp.zeros((1,), gate.dtype)])
    sent_hidden = hidden_rows[source_route].reshape(groups, block_rows, hidden_width)
    sent_gate = gate_rows[source_route].reshape(groups, block_rows)
    padded_grad = jnp.concatenate([out_grad, jnp.zeros((1, model_width), out_grad.dtype)], axis=0)
    token_rows = jnp.where(source_route < route_count, source_route // chosen_count, tok_rows)
    sent_grad = padded_grad[token_rows].reshape(groups, block_rows, model_width)
    got_grad, got_hidden, got_gate = (
        lax.all_to_all(sent_grad, "expert", split_axis=0, concat_axis=0, tiled=True),
        lax.all_to_all(sent_hidden, "expert", split_axis=0, concat_axis=0, tiled=True),
        lax.all_to_all(sent_gate, "expert", split_axis=0, concat_axis=0, tiled=True),
    )
    weights = down_weight[0]
    grad_four = got_grad.reshape(groups, slots, capacity, model_width)
    hidden_four = got_hidden.reshape(groups, slots, capacity, hidden_width)
    gate_four = got_gate.reshape(groups, slots, capacity).astype(jnp.float32)[..., None]
    projected = jnp.einsum("xscd,sfd->xscf", grad_four, weights, preferred_element_type=jnp.float32)
    back_rows = (
        (gate_four * projected).astype(jnp.bfloat16).reshape(groups, block_rows, hidden_width)
    )
    back_gate = (
        jnp.sum(hidden_four.astype(jnp.float32) * projected, axis=-1)
        .astype(jnp.bfloat16)
        .reshape(groups, block_rows)
    )
    came_rows, came_gate = (
        lax.all_to_all(back_rows, "expert", split_axis=0, concat_axis=0, tiled=True),
        lax.all_to_all(back_gate, "expert", split_axis=0, concat_axis=0, tiled=True),
    )
    d_hidden = came_rows.reshape(length, hidden_width)[places].reshape(
        tok_rows, chosen_count, hidden_width
    )
    d_gate = came_gate.reshape(length)[places].reshape(tok_rows, chosen_count)
    scaled = (gate_four * hidden_four.astype(jnp.float32)).astype(jnp.bfloat16)
    partial_value = jnp.einsum(
        "xscf,xscd->sfd", scaled, grad_four, preferred_element_type=jnp.float32
    )
    dp_count = lax.axis_size("dp")
    shares = lax.all_to_all(partial_value, "dp", split_axis=1, concat_axis=0, tiled=True)
    group_sum = jnp.sum(
        shares.reshape(dp_count, slots, hidden_width // dp_count, model_width), axis=0
    )
    own_slots = lax.dynamic_slice_in_dim(flat_slots, own_index * slots, slots)
    expert_ids = jnp.arange(EXPERTS, dtype=jnp.int32)
    copies = jnp.sum((flat_slots[:, None] == expert_ids[None, :]).astype(jnp.int32), axis=0)
    is_hot = copies >= 2
    hot_rank = jnp.cumsum(is_hot.astype(jnp.int32)) - 1
    picks = own_slots[:, None] == expert_ids[None, :]
    slot_hot = jnp.any(picks & is_hot[None, :], axis=1)
    slot_rank = jnp.sum(jnp.where(picks, hot_rank[None, :], 0), axis=1)
    member = (slot_rank[:, None] == jnp.arange(HOT, dtype=jnp.int32)[None, :]) & slot_hot[:, None]
    hot_table = jnp.sum(jnp.where(member[:, :, None, None], group_sum[:, None], 0.0), axis=0)
    hot_total = lax.psum(hot_table, "expert")
    from_table = jnp.sum(jnp.where(member[:, :, None, None], hot_total[None], 0.0), axis=1)
    d_weight = jnp.where(slot_hot[:, None, None], from_table, group_sum)[None]
    return (d_hidden, d_gate, d_weight)


def solution(mesh):
    placed = (
        P(("dp", "expert"), None),
        P(("dp", "expert"), None, None),
        P(("dp", "expert"), None),
        P(("dp", "expert"), None),
        P(("dp", "expert"), None),
        P(),
        P("expert", None, None, None),
    )
    return jax.shard_map(
        per_device,
        mesh=mesh,
        in_specs=placed,
        out_specs=(
            P(("dp", "expert"), None, None),
            P(("dp", "expert"), None),
            P("expert", None, "dp", None),
        ),
        check_vma=False,
    )
```

profile of v0, /device:TPU:64, one launch (start us, length us, event | category | flops | bytes accessed | tf_op | source)
XLA Modules:
  0.0 556.7 jit_solution(8288861238006414382)
XLA Ops:
  11.2 27.0 %reduce-window.18 = s32[96,8,128]{2,1,0:T(8,128)S(1)} reduce-window(s32[96,8,128]{2,1,0:T(8,128)S(1)} %fusion.14, s32[]{:T(128)} %constant.20.clone.1), window={size=1x1x128 pad=0_0x0_0x127_0}, to_apply=%region_2.3 | reduce-window | flops 12484608 | bytes 786436 | tf_op jit(solution)/shard_map/reduce-window
  39.6 4.3 scatter_custom_fusion
  44.0 9.5 %gather_fusion = bf16[1536]{0:T(1024)(128)(2,1)S(1)} fusion(bf16[1025]{0:T(1024)(128)(2,1)S(1)} %pad_maximum_fusion, s32[2048]{0:T(1024)S(1)} %get-tuple-element.28), kind=kCustom, calls=%fused_computation | custom fusion | bytes 12288 | tf_op jit(solution)/shard_map/gather | solution.py:63
  54.2 9.9 %all-to-all-start = ((bf16[32,1,48]{2,1,0:T(2,128)(2,1)}), bf16[32,1,48]{2,1,0:T(2,128)(2,1)S(1)}, u32[]{:S(2)}, u32[]{:S(2)}) async-start(bf16[32,1,48]{2,1,0:T(2,128)(2,1)} %all_to_all.36), calls=%async_computation | async-start | bytes 32768 | tf_op jit(solution)/shard_map/all_to_all | solution.py:70
  64.1 1.2 concatenate.11
  65.3 5.3 gather_fusion.3
  70.6 3.2 all-to-all-done
  73.9 6.8 %all-to-all-start.3 = ((bf16[32,48,384]{2,1,0:T(8,128)(2,1)}), bf16[32,48,384]{2,1,0:T(8,128)(2,1)}, u32[]{:S(2)}, u32[]{:S(2)}) async-start(bf16[32,48,384]{2,1,0:T(8,128)(2,1)} %bitcast.60), calls=%async_computation.3 | async-start | bytes 2359296 | tf_op jit(solution)/shard_map/all_to_all | solution.py:69
  80.7 5.8 %gather_fusion.1 = bf16[1536,1024]{1,0:T(8,128)(2,1)} fusion(bf16[129,1024]{1,0:T(8,128)(2,1)S(1)} %concatenate.10, s32[2048]{0:T(1024)S(1)} %get-tuple-element.27), kind=kCustom, calls=%fused_computation.1 | custom fusion | bytes 6297600 | tf_op jit(solution)/shard_map/gather | solution.py:66
  86.6 25.1 %all-to-all-done.3 = bf16[32,48,384]{2,1,0:T(8,128)(2,1)} async-done(((bf16[32,48,384]{2,1,0:T(8,128)(2,1)}), bf16[32,48,384]{2,1,0:T(8,128)(2,1)}, u32[]{:S(2)}, u32[]{:S(2)}) %all-to-all-start.3) | async-done | bytes 1179680 | tf_op jit(solution)/shard_map/all_to_all | solution.py:69
  111.6 5.1 all-to-all-start.1
  117.6 73.3 %all-to-all-done.1 = bf16[32,48,1024]{2,1,0:T(8,128)(2,1)} async-done(((bf16[32,48,1024]{2,1,0:T(8,128)(2,1)}), bf16[32,48,1024]{2,1,0:T(8,128)(2,1)}, u32[]{:S(2)}, u32[]{:S(2)}) %all-to-all-start.1) | async-done | bytes 3145760 | tf_op jit(solution)/shard_map/all_to_all | solution.py:68
  190.9 4.7 fusion.6
  197.1 5.4 all-to-all-start.4
  202.6 3.8 fusion.7
  206.3 5.9 %copy.125 = f32[3,384,1024]{2,0,1:T(4,128)} copy(f32[3,384,1024]{2,1,0:T(8,128)S(1)} %fusion.7) | data formatting | bytes 9437184 | tf_op jit(solution)/shard_map/xscf,xscd->sfd/dot_general | solution.py:94
  212.2 10.0 %all-to-all-start.5 = ((f32[3,384,1024]{2,0,1:T(4,128)}), f32[3,384,1024]{2,0,1:T(4,128)}, u32[]{:S(2)}, u32[]{:S(2)}) async-start(f32[3,384,1024]{2,0,1:T(4,128)} %copy.125), calls=%async_computation.5 | async-start | bytes 12582912 | tf_op jit(solution)/shard_map/all_to_all | solution.py:98
  223.5 1.4 copy.122
  224.9 1.4 reduce-window.20
  226.3 1.2 dynamic_slice.3
  228.8 130.7 %all-to-all-done.5 = f32[3,384,1024]{2,0,1:T(4,128)} async-done(((f32[3,384,1024]{2,0,1:T(4,128)}), f32[3,384,1024]{2,0,1:T(4,128)}, u32[]{:S(2)}, u32[]{:S(2)}) %all-to-all-start.5) | async-done | bytes 4718624 | tf_op jit(solution)/shard_map/all_to_all | solution.py:98
  359.5 9.6 %all-to-all-start.2 = ((bf16[32,48,384]{2,1,0:T(8,128)(2,1)}), bf16[32,48,384]{2,1,0:T(8,128)(2,1)S(1)}, u32[]{:S(2)}, u32[]{:S(2)}) async-start(bf16[32,48,384]{2,1,0:T(8,128)(2,1)} %bitcast.61), calls=%async_computation.2 | async-start | bytes 2359296 | tf_op jit(solution)/shard_map/all_to_all | solution.py:86
  372.9 5.3 reduce_sum.91
  379.4 2.5 select_reduce_fusion.1
  381.9 1.3 broadcast_clamp_fusion
  384.6 6.9 %gather_fusion.4 = bf16[1024]{0:T(1024)(128)(2,1)S(1)} fusion(bf16[1536]{0:T(1024)(128)(2,1)S(1)} %reshape.219, s32[1024]{0:T(1024)} %broadcast_clamp_fusion), kind=kCustom, calls=%fused_computation.4 | custom fusion | bytes 8192 | tf_op jit(solution)/shard_map/gather | solution.py:92
  392.2 1.4 copy.128
  393.6 7.3 %all-to-all-done.2 = bf16[32,48,384]{2,1,0:T(8,128)(2,1)S(1)} async-done(((bf16[32,48,384]{2,1,0:T(8,128)(2,1)}), bf16[32,48,384]{2,1,0:T(8,128)(2,1)S(1)}, u32[]{:S(2)}, u32[]{:S(2)}) %all-to-all-start.2) | async-done | bytes 1179680 | tf_op jit(solution)/shard_map/all_to_all | solution.py:86
  401.0 5.4 gather_fusion.2
  406.4 139.3 %all-reduce.4.cloned.1.call-done = f32[16,24,1024]{2,1,0:T(8,128)} async-done(((f32[16,24,1024]{2,1,0:T(8,128)}), f32[16,24,1024]{2,1,0:T(8,128)}) %all-reduce.4.cloned.1.call-update) | async-done | bytes 1572880 | tf_op jit(solution)/shard_map/psum | solution.py:112
  545.7 1.9 select_reduce_fusion
  547.7 1.3 bitcast_select_fusion
  (59 shorter events, 18.9 us)
Async XLA Ops:
  7.2 183.7 %copy-start = (bf16[1,3,384,1024]{3,2,1,0:T(8,128)(2,1)S(1)}, bf16[1,3,384,1024]{3,2,1,0:T(8,128)(2,1)}, u32[]{:S(2)}) copy-start(bf16[1,3,384,1024]{3,2,1,0:T(8,128)(2,1)} %param.13) | copy-start | bytes 7077892
  10.9 27.4 %copy-start.3 = (s32[96]{0:T(128)}, s32[96]{0:T(128)S(1)}, u32[]{:S(2)}) copy-start(s32[96]{0:T(128)S(1)} %eq.109) | copy-start | bytes 1156
  39.1 0.6 copy-start.2
  54.2 19.7 %all-to-all-start = ((bf16[32,1,48]{2,1,0:T(2,128)(2,1)}), bf16[32,1,48]{2,1,0:T(2,128)(2,1)S(1)}, u32[]{:S(2)}, u32[]{:S(2)}) async-start(bf16[32,1,48]{2,1,0:T(2,128)(2,1)} %all_to_all.36), calls=%async_computation | async-start | bytes 32768 | tf_op jit(solution)/shard_map/all_to_all | solution.py:70
  70.6 10.0 %copy-start.1 = (bf16[128,1024]{1,0:T(8,128)(2,1)S(1)}, bf16[128,1024]{1,0:T(8,128)(2,1)}, u32[]{:S(2)}) copy-start(bf16[128,1024]{1,0:T(8,128)(2,1)} %param.7) | copy-start | bytes 786436
  73.9 37.8 %all-to-all-start.3 = ((bf16[32,48,384]{2,1,0:T(8,128)(2,1)}), bf16[32,48,384]{2,1,0:T(8,128)(2,1)}, u32[]{:S(2)}, u32[]{:S(2)}) async-start(bf16[32,48,384]{2,1,0:T(8,128)(2,1)} %bitcast.60), calls=%async_computation.3 | async-start | bytes 2359296 | tf_op jit(solution)/shard_map/all_to_all | solution.py:69
  111.6 79.2 %all-to-all-start.1 = ((bf16[32,48,1024]{2,1,0:T(8,128)(2,1)}), bf16[32,48,1024]{2,1,0:T(8,128)(2,1)}, u32[]{:S(2)}, u32[]{:S(2)}) async-start(bf16[32,48,1024]{2,1,0:T(8,128)(2,1)} %bitcast.59), calls=%async_computation.1 | async-start | bytes 6291456 | tf_op jit(solution)/shard_map/all_to_all | solution.py:68
  197.1 15.1 %all-to-all-start.4 = ((bf16[32,1,48]{2,1,0:T(2,128)(2,1)}), bf16[32,1,48]{2,1,0:T(2,128)(2,1)S(1)}, u32[]{:S(2)}, u32[]{:S(2)}) async-start(bf16[32,1,48]{2,1,0:T(2,128)(2,1)} %copy.121), calls=%async_computation.4 | async-start | bytes 32768 | tf_op jit(solution)/shard_map/all_to_all | solution.py:87
  212.2 147.3 %all-to-all-start.5 = ((f32[3,384,1024]{2,0,1:T(4,128)}), f32[3,384,1024]{2,0,1:T(4,128)}, u32[]{:S(2)}, u32[]{:S(2)}) async-start(f32[3,384,1024]{2,0,1:T(4,128)} %copy.125), calls=%async_computation.5 | async-start | bytes 12582912 | tf_op jit(solution)/shard_map/all_to_all | solution.py:98
  359.5 41.5 %all-to-all-start.2 = ((bf16[32,48,384]{2,1,0:T(8,128)(2,1)}), bf16[32,48,384]{2,1,0:T(8,128)(2,1)S(1)}, u32[]{:S(2)}, u32[]{:S(2)}) async-start(bf16[32,48,384]{2,1,0:T(8,128)(2,1)} %bitcast.61), calls=%async_computation.2 | async-start | bytes 2359296 | tf_op jit(solution)/shard_map/all_to_all | solution.py:86
  369.1 176.6 %all-reduce.4.cloned.1.call-start = ((), (), s32[]{:S(2)}) async-start(), calls=%async_computation.6 | async-start | bytes 3145728 | tf_op jit(solution)/shard_map/psum | solution.py:112
  371.7 0.6 copy-start.5
  401.0 144.8 %copy-start.4 = (pred[3,16]{1,0:T(4,128)(4,1)S(1)}, pred[3,16]{1,0:T(4,128)(4,1)}, u32[]{:S(2)}) copy-start(pred[3,16]{1,0:T(4,128)(4,1)} %fusion.23) | copy-start | bytes 148
  401.0 146.7 %copy-start.6 = (pred[3]{0:T(512)(128)(4,1)S(1)}, pred[3]{0:T(512)(128)(4,1)}, u32[]{:S(2)}) copy-start(pred[3]{0:T(512)(128)(4,1)} %copy-done.5) | copy-start | bytes 13
Sparse Core Ops, SparseCore 0:
  382.0 163.6 all-reduce.3
where the time goes:
time: 558 us; the launch traced here: 557 us
  waiting for transfers between devices  379 us (68%)
  local copies, waits for them, and re-layouts  61.4 us (11%)
  starting transfers between devices  46.9 us (8%)
  other arithmetic  46.5 us (8%)
  between operations  14.3 us (3%)
  matrix products  8.51 us (2%)
    psum x1, waiting for transfers between devices, per_device(): hot_total = lax.psum(hot_table, 'expert')  139 us
    all_to_all x1, waiting for transfers between devices, per_device(): lax.all_to_all(partial_value, 'dp', split_axis=1, concat_axis=0, tiled=True)  131 us
    all_to_all x1, waiting for transfers between devices, per_device(): lax.all_to_all(sent_grad, 'expert', split_axis=0, concat_axis=0, tiled=True)  73.3 us
    another operation x4, other arithmetic  28.6 us
    all_to_all x1, waiting for transfers between devices, per_device(): lax.all_to_all(sent_hidden, 'expert', split_axis=0, concat_axis=0, tiled=...  25.1 us
  transfers between devices with their start and end apart: 7, of which 6 were waited for; matrix products, arithmetic and copies ran while one was open for 11% of the time, Pallas kernels for 0%

commit v1 on v0

--- a/solution.py
+++ b/solution.py
@@ -2,6 +2,7 @@
 import jax.numpy as jnp
 from jax import lax
 from jax.sharding import PartitionSpec as P
+from jax.lax import all_gather
 
 EXPERTS = 64
 CAP = 16
@@ -109,7 +110,7 @@
     slot_rank = jnp.sum(jnp.where(picks, hot_rank[None, :], 0), axis=1)
     member = (slot_rank[:, None] == jnp.arange(HOT, dtype=jnp.int32)[None, :]) & slot_hot[:, None]
     hot_table = jnp.sum(jnp.where(member[:, :, None, None], group_sum[:, None], 0.0), axis=0)
-    hot_total = lax.psum(hot_table, "expert")
+    hot_total = jnp.sum(all_gather(hot_table, "expert"), axis=0)
     from_table = jnp.sum(jnp.where(member[:, :, None, None], hot_total[None], 0.0), axis=1)
     d_weight = jnp.where(slot_hot[:, None, None], from_table, group_sum)[None]
     return (d_hidden, d_gate, d_weight)

time: 558 us -> 743 us (1.33)
  the two profiles are of different devices: /device:TPU:64 before, /device:TPU:1 now
where the time goes in v1:
time: 743 us; the launch traced here: 742 us
  waiting for transfers between devices  556 us (75%)
  local copies, waits for them, and re-layouts  57.7 us (8%)
  other arithmetic  57.4 us (8%)
  starting transfers between devices  48 us (6%)
  between operations  14.3 us (2%)
  matrix products  8.83 us (1%)
    all_gather x1, waiting for transfers between devices, per_device(): hot_total = jnp.sum(all_gather(hot_table, 'expert'), axis=0)  287 us
    all_to_all x1, waiting for transfers between devices, per_device(): lax.all_to_all(partial_value, 'dp', split_axis=1, concat_axis=0, tiled=True)  137 us
    all_to_all x1, waiting for transfers between devices, per_device(): lax.all_to_all(sent_grad, 'expert', split_axis=0, concat_axis=0, tiled=True)  73 us
    all_to_all x1, waiting for transfers between devices, per_device(): lax.all_to_all(back_rows, 'expert', split_axis=0, concat_axis=0, tiled=True)  29 us
    another operation x4, other arithmetic  27.3 us
    all_to_all x1, waiting for transfers between devices, per_device(): lax.all_to_all(sent_hidden, 'expert', split_axis=0, concat_axis=0, tiled=...  21.9 us
    reduce_sum x1, other arithmetic, per_device(): hot_total = jnp.sum(all_gather(hot_table, 'expert'), axis=0)  18.5 us
  transfers between devices with their start and end apart: 7, of which 7 were waited for; matrix products, arithmetic and copies ran while one was open for 5% of the time, Pallas kernels for 0%

profile of v1, /device:TPU:1, one launch (start us, length us, event | category | flops | bytes accessed | tf_op | source)
XLA Modules:
  0.0 742.1 jit_solution(17253268308082516138)
XLA Ops:
  7.2 0.9 copy.110
  11.2 27.0 %reduce-window.18 = s32[96,8,128]{2,1,0:T(8,128)S(1)} reduce-window(s32[96,8,128]{2,1,0:T(8,128)S(1)} %fusion.14, s32[]{:T(128)} %constant.20.clone.1), window={size=1x1x128 pad=0_0x0_0x127_0}, to_apply=%region_2.3 | reduce-window | flops 12484608 | bytes 786436 | tf_op jit(solution)/shard_map/reduce-window
  39.6 4.3 scatter_custom_fusion
  44.0 9.5 %gather_fusion = bf16[1536]{0:T(1024)(128)(2,1)S(1)} fusion(bf16[1025]{0:T(1024)(128)(2,1)S(1)} %pad_maximum_fusion, s32[2048]{0:T(1024)S(1)} %get-tuple-element.28), kind=kCustom, calls=%fused_computation | custom fusion | bytes 12288 | tf_op jit(solution)/shard_map/gather | solution.py:64
  54.2 10.5 %all-to-all-start = ((bf16[32,1,48]{2,1,0:T(2,128)(2,1)}), bf16[32,1,48]{2,1,0:T(2,128)(2,1)S(1)}, u32[]{:S(2)}, u32[]{:S(2)}) async-start(bf16[32,1,48]{2,1,0:T(2,128)(2,1)} %all_to_all.36), calls=%async_computation | async-start | bytes 32768 | tf_op jit(solution)/shard_map/all_to_all | solution.py:71
  64.7 1.2 concatenate.11
  65.9 5.3 gather_fusion.3
  71.2 2.1 all-to-all-done
  73.3 7.4 all-to-all-start.3
  80.7 5.8 gather_fusion.1
  86.5 21.9 %all-to-all-done.3 = bf16[32,48,384]{2,1,0:T(8,128)(2,1)} async-done(((bf16[32,48,384]{2,1,0:T(8,128)(2,1)}), bf16[32,48,384]{2,1,0:T(8,128)(2,1)}, u32[]{:S(2)}, u32[]{:S(2)}) %all-to-all-start.3) | async-done | bytes 1179680 | tf_op jit(solution)/shard_map/all_to_all | solution.py:70
  108.5 8.3 %all-to-all-start.1 = ((bf16[32,48,1024]{2,1,0:T(8,128)(2,1)}), bf16[32,48,1024]{2,1,0:T(8,128)(2,1)}, u32[]{:S(2)}, u32[]{:S(2)}) async-start(bf16[32,48,1024]{2,1,0:T(8,128)(2,1)} %bitcast.62), calls=%async_computation.1 | async-start | bytes 6291456 | tf_op jit(solution)/shard_map/all_to_all | solution.py:69
  117.0 73.0 %all-to-all-done.1 = bf16[32,48,1024]{2,1,0:T(8,128)(2,1)} async-done(((bf16[32,48,1024]{2,1,0:T(8,128)(2,1)}), bf16[32,48,1024]{2,1,0:T(8,128)(2,1)}, u32[]{:S(2)}, u32[]{:S(2)}) %all-to-all-start.1) | async-done | bytes 3145760 | tf_op jit(solution)/shard_map/all_to_all | solution.py:69
  190.0 3.8 fusion.7
  193.8 5.9 copy.125
  199.7 12.7 %all-to-all-start.5 = ((f32[3,384,1024]{2,0,1:T(4,128)}), f32[3,384,1024]{2,0,1:T(4,128)}, u32[]{:S(2)}, u32[]{:S(2)}) async-start(f32[3,384,1024]{2,0,1:T(4,128)} %copy.125), calls=%async_computation.5 | async-start | bytes 12582912 | tf_op jit(solution)/shard_map/all_to_all | solution.py:99
  213.9 136.9 %all-to-all-done.5 = f32[3,384,1024]{2,0,1:T(4,128)} async-done(((f32[3,384,1024]{2,0,1:T(4,128)}), f32[3,384,1024]{2,0,1:T(4,128)}, u32[]{:S(2)}, u32[]{:S(2)}) %all-to-all-start.5) | async-done | bytes 4718624 | tf_op jit(solution)/shard_map/all_to_all | solution.py:99
  350.8 4.5 reduce_sum.100
  355.5 1.8 select_reduce_fusion.1
  357.3 5.1 fusion.6
  363.2 5.0 all-to-all-start.4
  368.2 2.6 copy.118
  370.7 6.1 all-to-all-done.4
  376.8 3.9 all-to-all-start.2
  380.8 1.3 broadcast_clamp_fusion
  383.5 6.9 gather_fusion.4
  391.1 1.4 copy.128
  392.5 29.0 %all-to-all-done.2 = bf16[32,48,384]{2,1,0:T(8,128)(2,1)S(1)} async-done(((bf16[32,48,384]{2,1,0:T(8,128)(2,1)}), bf16[32,48,384]{2,1,0:T(8,128)(2,1)S(1)}, u32[]{:S(2)}, u32[]{:S(2)}) %all-to-all-start.2) | async-done | bytes 1179680 | tf_op jit(solution)/shard_map/all_to_all | solution.py:87
  421.5 5.3 gather_fusion.2
  426.8 286.7 %all-gather.3.cloned.1.call-done = f32[512,24,1024]{2,1,0:T(8,128)} async-done(((f32[16,24,1024]{2,1,0:T(8,128)}), f32[512,24,1024]{2,1,0:T(8,128)}) %all-gather.3.cloned.1.call-update) | async-done | bytes 50331664 | tf_op jit(solution)/shard_map/all_gather | solution.py:113
  713.5 18.5 %reduce_sum.102 = f32[16,24,1024]{2,1,0:T(8,128)} reduce(f32[32,16,24,1024]{3,2,1,0:T(8,128)} %bitcast.60, f32[]{:T(128)} %constant.53.clone.1), dimensions={0}, to_apply=%region_13.14 | reduce | flops 12189696 | bytes 51904516 | tf_op jit(solution)/shard_map/reduce_sum | solution.py:113
  732.1 1.9 select_reduce_fusion
  (64 shorter events, 11.2 us)
Async XLA Ops:
  7.2 350.1 %copy-start = (bf16[1,3,384,1024]{3,2,1,0:T(8,128)(2,1)S(1)}, bf16[1,3,384,1024]{3,2,1,0:T(8,128)(2,1)}, u32[]{:S(2)}) copy-start(bf16[1,3,384,1024]{3,2,1,0:T(8,128)(2,1)} %param.13) | copy-start | bytes 7077892
  39.0 0.6 copy-start.4
  54.2 19.1 %all-to-all-start = ((bf16[32,1,48]{2,1,0:T(2,128)(2,1)}), bf16[32,1,48]{2,1,0:T(2,128)(2,1)S(1)}, u32[]{:S(2)}, u32[]{:S(2)}) async-start(bf16[32,1,48]{2,1,0:T(2,128)(2,1)} %all_to_all.36), calls=%async_computation | async-start | bytes 32768 | tf_op jit(solution)/shard_map/all_to_all | solution.py:71
  71.2 9.5 %copy-start.3 = (bf16[128,1024]{1,0:T(8,128)(2,1)S(1)}, bf16[128,1024]{1,0:T(8,128)(2,1)}, u32[]{:S(2)}) copy-start(bf16[128,1024]{1,0:T(8,128)(2,1)} %param.7) | copy-start | bytes 786436
  73.3 35.2 %all-to-all-start.3 = ((bf16[32,48,384]{2,1,0:T(8,128)(2,1)}), bf16[32,48,384]{2,1,0:T(8,128)(2,1)}, u32[]{:S(2)}, u32[]{:S(2)}) async-start(bf16[32,48,384]{2,1,0:T(8,128)(2,1)} %bitcast.63), calls=%async_computation.3 | async-start | bytes 2359296 | tf_op jit(solution)/shard_map/all_to_all | solution.py:70
  108.5 81.5 %all-to-all-start.1 = ((bf16[32,48,1024]{2,1,0:T(8,128)(2,1)}), bf16[32,48,1024]{2,1,0:T(8,128)(2,1)}, u32[]{:S(2)}, u32[]{:S(2)}) async-start(bf16[32,48,1024]{2,1,0:T(8,128)(2,1)} %bitcast.62), calls=%async_computation.1 | async-start | bytes 6291456 | tf_op jit(solution)/shard_map/all_to_all | solution.py:69
  199.7 151.1 %all-to-all-start.5 = ((f32[3,384,1024]{2,0,1:T(4,128)}), f32[3,384,1024]{2,0,1:T(4,128)}, u32[]{:S(2)}, u32[]{:S(2)}) async-start(f32[3,384,1024]{2,0,1:T(4,128)} %copy.125), calls=%async_computation.5 | async-start | bytes 12582912 | tf_op jit(solution)/shard_map/all_to_all | solution.py:99
  212.3 501.2 %all-gather.3.cloned.1.call-start = ((), (), s32[]{:S(2)}) async-start(), calls=%async_computation.6 | async-start | bytes 51904512 | tf_op jit(solution)/shard_map/all_gather | solution.py:113
  213.2 0.5 copy-start.7
  213.9 141.6 %copy-start.5 = (pred[3,16]{1,0:T(4,128)(4,1)}, pred[3,16]{1,0:T(4,128)(4,1)S(1)}, u32[]{:S(2)}) copy-start(pred[3,16]{1,0:T(4,128)(4,1)S(1)} %fusion.23) | copy-start | bytes 148
  355.3 7.1 copy-start.1
  363.2 13.6 %all-to-all-start.4 = ((bf16[32,1,48]{2,1,0:T(2,128)(2,1)}), bf16[32,1,48]{2,1,0:T(2,128)(2,1)S(1)}, u32[]{:S(2)}, u32[]{:S(2)}) async-start(bf16[32,1,48]{2,1,0:T(2,128)(2,1)} %copy.121), calls=%async_computation.4 | async-start | bytes 32768 | tf_op jit(solution)/shard_map/all_to_all | solution.py:88
  376.8 44.7 %all-to-all-start.2 = ((bf16[32,48,384]{2,1,0:T(8,128)(2,1)}), bf16[32,48,384]{2,1,0:T(8,128)(2,1)S(1)}, u32[]{:S(2)}, u32[]{:S(2)}) async-start(bf16[32,48,384]{2,1,0:T(8,128)(2,1)} %bitcast.64), calls=%async_computation.2 | async-start | bytes 2359296 | tf_op jit(solution)/shard_map/all_to_all | solution.py:87
  713.5 18.5 %copy-start.6 = (pred[3,16]{1,0:T(4,128)(4,1)S(1)}, pred[3,16]{1,0:T(4,128)(4,1)}, u32[]{:S(2)}) copy-start(pred[3,16]{1,0:T(4,128)(4,1)} %copy-done.5) | copy-start | bytes 148
  713.5 20.5 %copy-start.2 = (f32[3,24,1024]{2,0,1:T(4,128)S(1)}, f32[3,24,1024]{2,0,1:T(4,128)}, u32[]{:S(2)}) copy-start(f32[3,24,1024]{2,0,1:T(4,128)} %copy-done.1) | copy-start | bytes 884740
  713.5 20.5 %copy-start.8 = (pred[3]{0:T(512)(128)(4,1)S(1)}, pred[3]{0:T(512)(128)(4,1)}, u32[]{:S(2)}) copy-start(pred[3]{0:T(512)(128)(4,1)} %copy-done.7) | copy-start | bytes 13
Sparse Core Ops, SparseCore 0:
  357.4 356.0 all-gather.2
